TPU v7x, 32 devices: a whole 2x2x4 slice. The times are simulated.
32 devices in a mesh: seq: 8 (over z, y), head: 4 (over x, core).
Axes of the slice: x: 2, y: 2, z: 4, core: 2. Of those that a mesh axis runs over, the one named last changes fastest.
Arguments:
- query: bfloat16 [12288, 3072], P(('seq', 'head')), may hold values from -40 to 40
- key: bfloat16 [12288, 3072], P(('seq', 'head')), may hold values from -4 to 4
- value: bfloat16 [12288, 3072], P(('seq', 'head')), may hold values from -6 to 6
- raster_to_tile: int32 [12288], P(('seq', 'head')), may hold values from 0 to 12287, as said below
- window_list: int32 [32, 4], P('seq'), may hold values from 0 to 31, as said below
- valid_count: int32 [32], replicated, may hold values from 96 to 384
Outputs:
- attended: bfloat16 [12288, 3072], P(('seq', 'head'))
Inputs may be any that keep to these rules, and one draw needn't show every extreme that they name: `raster_to_tile`: A permutation of the slots. Raster shard d (rows d * 1536 // 4 onward, d counting seq+head) holds exactly 48 slots of every owner o, where owner o holds slots o * 1536 to (o+1) * 1536 - 1. `window_list`: row t holds t first, then 4 - 1 distinct other tiles, each within 3 tiles of t.
All inputs are finite; a program needn't handle non-finite values.
Results may differ from a plain program's by a relative error of at most 0.0036.
Values may be sent and summed in bfloat16 or wider, within the bound.
No kernel may reach another device: no remote copies, remote signals or barrier semaphores. Data moves between devices by JAX's collectives and lax.ppermute only.
A program may use at most 128 MiB of HBM per device.

v0:
```python
import jax
import jax.numpy as jnp
from jax import lax
from jax.sharding import PartitionSpec as P

HEAD_DIM = 128


def body(query, key, value, raster_to_tile, window_list, valid_count):
    seq_count = lax.axis_size("seq")
    head_count = lax.axis_size("head")
    seq_pos = lax.axis_index("seq")
    rows_here, width = query.shape
    part_width = width // head_count
    tile_dev, win = window_list.shape
    tok_dev = rows_here * head_count
    tile = tok_dev // tile_dev
    share = rows_here // seq_count
    reach = win - 1
    rim = reach * tile
    ext_rows = tok_dev + 2 * rim
    ext_tiles = tile_dev + 2 * reach
    heads_here = part_width // HEAD_DIM
    all_tiles = valid_count.shape[0]
    order = jnp.argsort(raster_to_tile)
    slots_sorted = raster_to_tile[order].reshape(seq_count, share)
    query_sorted = query[order].reshape(seq_count, share, head_count, part_width)
    joined = jnp.concatenate(
        [
            key.reshape(rows_here, head_count, part_width),
            value.reshape(rows_here, head_count, part_width),
        ],
        axis=2,
    )
    pair_sorted = joined[order].reshape(seq_count, share, head_count, 2 * part_width)
    zero_pair = jnp.zeros_like(pair_sorted[:1])
    wide_pair = jnp.concatenate(
        [
            jnp.concatenate([zero_pair, pair_sorted[:-1]], axis=0),
            pair_sorted,
            jnp.concatenate([pair_sorted[1:], zero_pair], axis=0),
        ],
        axis=1,
    )
    empty_slots = jnp.full((1, share), -1, jnp.int32)
    wide_slots = jnp.concatenate(
        [
            jnp.concatenate([empty_slots, slots_sorted[:-1]], axis=0),
            slots_sorted,
            jnp.concatenate([slots_sorted[1:], empty_slots], axis=0),
        ],
        axis=1,
    )
    slot_send = jnp.broadcast_to(wide_slots[:, :, None], (seq_count, 3 * share, head_count))
    query_in, pair_in, slot_in = (
        lax.all_to_all(
            lax.all_to_all(query_sorted, "seq", split_axis=0, concat_axis=0, tiled=True),
            "head",
            split_axis=2,
            concat_axis=1,
            tiled=True,
        ),
        lax.all_to_all(
            lax.all_to_all(wide_pair, "seq", split_axis=0, concat_axis=0, tiled=True),
            "head",
            split_axis=2,
            concat_axis=1,
            tiled=True,
        ),
        lax.all_to_all(
            lax.all_to_all(slot_send, "seq", split_axis=0, concat_axis=0, tiled=True),
            "head",
            split_axis=2,
            concat_axis=1,
            tiled=True,
        ),
    )
    middle = slot_in.reshape(seq_count, head_count, 3, share)[:, :, 1, :]
    local = middle.reshape(tok_dev) - seq_pos * tok_dev
    place = jnp.zeros((tok_dev,), jnp.int32).at[local].set(jnp.arange(tok_dev, dtype=jnp.int32))
    query_tile = query_in.reshape(tok_dev, part_width)[place]
    every_slot = slot_in.reshape(3 * tok_dev)
    shifted = every_slot - (seq_pos * tok_dev - rim)
    target = jnp.where((every_slot >= 0) & (shifted >= 0) & (shifted < ext_rows), shifted, ext_rows)
    place_ext = (
        jnp.full((ext_rows,), 3 * tok_dev, jnp.int32)
        .at[target]
        .set(jnp.arange(3 * tok_dev, dtype=jnp.int32), mode="drop")
    )
    padded = jnp.concatenate(
        [
            pair_in.reshape(3 * tok_dev, 2 * part_width),
            jnp.zeros((1, 2 * part_width), pair_in.dtype),
        ],
        axis=0,
    )
    pair_ext = padded[place_ext]
    first_tile = seq_pos * tile_dev - reach
    global_tiles = jnp.clip(first_tile + jnp.arange(ext_tiles, dtype=jnp.int32), 0, all_tiles - 1)
    key_usable = jnp.arange(tile, dtype=jnp.int32)[None, :] < valid_count[global_tiles][:, None]
    own_usable = key_usable[reach : reach + tile_dev]
    local_windows = window_list - first_tile
    query_blocks = query_tile.reshape(tile_dev, tile, heads_here, HEAD_DIM)
    pair_blocks = pair_ext.reshape(ext_tiles, tile, 2, heads_here, HEAD_DIM)
    scale = HEAD_DIM ** (-0.5)

    def one_tile(item):
        query_blk, windows, query_usable = item
        picked = pair_blocks[windows]
        keys_blk = picked[:, :, 0].reshape(win * tile, heads_here, HEAD_DIM)
        values_blk = picked[:, :, 1].reshape(win * tile, heads_here, HEAD_DIM)
        usable = key_usable[windows].reshape(win * tile)
        scores = (
            jnp.einsum("qhd,khd->hqk", query_blk, keys_blk, preferred_element_type=jnp.float32)
            * scale
        )
        scores = jnp.where(usable[None, None, :], scores, -jnp.inf)
        top = jnp.max(scores, axis=2, keepdims=True)
        weights = jnp.exp(scores - top)
        total = jnp.sum(weights, axis=2)
        mixed = jnp.einsum(
            "hqk,khd->qhd",
            weights.astype(jnp.bfloat16),
            values_blk,
            preferred_element_type=jnp.float32,
        )
        mixed = mixed / jnp.transpose(total)[:, :, None]
        mixed = jnp.where(query_usable[:, None, None], mixed, 0.0)
        return mixed.astype(jnp.bfloat16).reshape(tile, part_width)

    out_tile = lax.map(one_tile, (query_blocks, local_windows, own_usable)).reshape(
        tok_dev, part_width
    )
    outgoing = out_tile[local].reshape(seq_count, head_count, share, 1, part_width)
    arrived = lax.all_to_all(
        lax.all_to_all(outgoing, "seq", split_axis=0, concat_axis=0, tiled=True),
        "head",
        split_axis=1,
        concat_axis=3,
        tiled=True,
    )
    sorted_rows = arrived.reshape(rows_here, width)
    inverse = (
        jnp.zeros((rows_here,), jnp.int32).at[order].set(jnp.arange(rows_here, dtype=jnp.int32))
    )
    return sorted_rows[inverse]


def solution(mesh):
    placed = (
        P(("seq", "head"), None),
        P(("seq", "head"), None),
        P(("seq", "head"), None),
        P(("seq", "head")),
        P("seq", None),
        P(),
    )
    return jax.shard_map(
        body, mesh=mesh, in_specs=placed, out_specs=P(("seq", "head"), None), check_vma=False
    )
```

profile of v0, /device:TPU:0, one launch (start us, length us, event | category | flops | bytes accessed | tf_op | source)
XLA Modules:
  0.0 936.3 jit_solution(2303994051912508373)
XLA Ops:
  9.2 13.8 %all_to_all.80 = s32[8,144,4]{1,2,0:T(4,128)S(1)} all-to-all(s32[8,144,4]{1,2,0:T(4,128)S(1)} %broadcast_in_dim.78), channel_id=1, replica_groups=mesh['seq'=8,'head'=4] {'seq'}, dimensions={0} | all-to-all | bytes 36864 | tf_op jit(solution)/shard_map/all_to_all | solution.py:71
  51.7 6.6 pad_maximum_fusion
  58.3 19.9 %gather_fusion.3 = bf16[384,4,1536]{2,1,0:T(4,128)(2,1)} fusion(bf16[384,4,1536]{2,1,0:T(4,128)(2,1)} %pad_maximum_fusion, s32[1024]{0:T(1024)S(1)} %pad_clamp_fusion.5), kind=kCustom, calls=%fused_computation.3 | custom fusion | bytes 9438720 | tf_op jit(solution)/shard_map/gather | solution.py:35
  102.3 305.1 %all-to-all-done = bf16[8,144,4,1536]{3,1,2,0:T(8,128)(2,1)} async-done(((bf16[8,144,4,1536]{3,1,2,0:T(8,128)(2,1)}), bf16[8,144,4,1536]{3,1,2,0:T(8,128)(2,1)}, u32[]{:S(2)}, u32[]{:S(2)}) %all-to-all-start) | async-done | bytes 14155808 | tf_op jit(solution)/shard_map/all_to_all | solution.py:64
  411.9 10.6 %copy.78 = bf16[8,144,4,1536]{3,1,0,2:T(8,128)(2,1)} copy(bf16[8,144,4,1536]{3,1,2,0:T(8,128)(2,1)} %all-to-all-done) | data formatting | bytes 28311552 | tf_op jit(solution)/shard_map/all_to_all | solution.py:64
  422.4 18.0 %all-to-all-done.5 = bf16[8,48,4,768]{3,1,0,2:T(8,128)(2,1)} async-done(((bf16[8,48,4,768]{3,1,0,2:T(8,128)(2,1)}), bf16[8,48,4,768]{3,1,0,2:T(8,128)(2,1)}, u32[]{:S(2)}, u32[]{:S(2)}) %all-to-all-start.5) | async-done | bytes 2359328 | tf_op jit(solution)/shard_map/all_to_all | solution.py:56
  454.7 17.4 %scatter_custom_fusion = s32[3840]{0:T(1024)S(1)} fusion(s32[4608]{0:T(1024)S(1)} %fusion.30, s32[4608]{0:T(1024)S(1)} %iota.23, s32[]{:T(128)} %constant.14.clone.1), kind=kCustom, calls=%fused_computation.61 | custom fusion | bytes 15364 | tf_op jit(solution)/shard_map/scatter | solution.py:88
  490.1 111.8 %all-to-all-done.1 = bf16[8,144,4,1536]{3,1,0,2:T(8,128)(2,1)} async-done(((bf16[8,144,4,1536]{3,1,0,2:T(8,128)(2,1)}), bf16[8,144,4,1536]{3,1,0,2:T(8,128)(2,1)}, u32[]{:S(2)}, u32[]{:S(2)}) %all-to-all-start.1) | async-done | bytes 14155808 | tf_op jit(solution)/shard_map/all_to_all | solution.py:63
  601.9 6.8 copy.79
  614.7 30.7 %gather_fusion.5 = bf16[3840,1536]{1,0:T(8,128)(2,1)} fusion(bf16[4609,1536]{1,0:T(8,128)(2,1)} %concatenate.28, s32[4096]{0:T(1024)S(1)} %pad_clamp_fusion.1), kind=kCustom, calls=%fused_computation.5 | custom fusion | bytes 23608320 | tf_op jit(solution)/shard_map/gather | solution.py:97
  645.4 24.3 %reshape.195 = bf16[10,384,2,6,128]{4,3,2,1,0:T(8,128)(2,1)} reshape(bf16[3840,1536]{1,0:T(8,128)(2,1)} %gather_fusion.5) | data formatting | bytes 23592960 | tf_op jit(solution)/shard_map/reshape | solution.py:104
  669.7 154.8 %while.11 = (s32[]{:T(128)}, bf16[4,384,768]{2,1,0:T(8,128)(2,1)}, pred[4,384]{1,0:T(4,128)(4,1)S(1)}, s32[4,4]{1,0:T(4,128)S(1)}, bf16[10,384,2,6,128]{4,3,2,1,...) while((s32[]{:T(128)}, bf16[4,384,768]{2,1,0:T(8,128)(2,1)}, ...), condition=%wide.region_6.7_spmd.clone, body=%wide.region_3.6_spmd.clone.sunk | while | flops 1851752704 | bytes 74384984 | solution.py:131
  670.6 9.5 %gather_fusion.1 = bf16[4,384,2,6,128]{4,3,2,1,0:T(8,128)(2,1)} fusion(bf16[10,384,2,6,128]{4,3,2,1,0:T(8,128)(2,1)} %get-tuple-element.197, s32[1024]{0:T(1024)S(1)} %pad_clamp_fusion.8), kind=kCustom, calls=%fused_computation.clone.clone.1 | custom fusion | bytes 9437200 | tf_op jit(solution)/shard_map/while/body/eval_jaxpr/gather | solution.py:109
  684.5 8.1 fusion.55
  692.6 7.9 fusion.56
  700.5 7.0 select_convert_fusion.2
  709.2 9.5 %gather_fusion.1 = bf16[4,384,2,6,128]{4,3,2,1,0:T(8,128)(2,1)} fusion(bf16[10,384,2,6,128]{4,3,2,1,0:T(8,128)(2,1)} %get-tuple-element.197, s32[1024]{0:T(1024)S(1)} %pad_clamp_fusion.8), kind=kCustom, calls=%fused_computation.clone.clone.1 | custom fusion | bytes 9437200 | tf_op jit(solution)/shard_map/while/body/eval_jaxpr/gather | solution.py:109
  723.1 8.1 fusion.55
  731.2 7.9 fusion.56
  739.1 7.0 select_convert_fusion.2
  747.9 9.5 %gather_fusion.1 = bf16[4,384,2,6,128]{4,3,2,1,0:T(8,128)(2,1)} fusion(bf16[10,384,2,6,128]{4,3,2,1,0:T(8,128)(2,1)} %get-tuple-element.197, s32[1024]{0:T(1024)S(1)} %pad_clamp_fusion.8), kind=kCustom, calls=%fused_computation.clone.clone.1 | custom fusion | bytes 9437200 | tf_op jit(solution)/shard_map/while/body/eval_jaxpr/gather | solution.py:109
  761.8 8.1 fusion.55
  769.9 7.9 fusion.56
  777.8 7.0 select_convert_fusion.2
  786.5 9.5 %gather_fusion.1 = bf16[4,384,2,6,128]{4,3,2,1,0:T(8,128)(2,1)} fusion(bf16[10,384,2,6,128]{4,3,2,1,0:T(8,128)(2,1)} %get-tuple-element.197, s32[1024]{0:T(1024)S(1)} %pad_clamp_fusion.8), kind=kCustom, calls=%fused_computation.clone.clone.1 | custom fusion | bytes 9437200 | tf_op jit(solution)/shard_map/while/body/eval_jaxpr/gather | solution.py:109
  800.4 8.1 fusion.55
  808.5 7.9 fusion.56
  816.4 7.0 select_convert_fusion.2
  824.5 8.1 gather_fusion.8
  832.6 57.1 %all_to_all.81 = bf16[8,4,48,1,768]{4,2,1,3,0:T(8,128)(2,1)S(1)} all-to-all(bf16[8,4,48,1,768]{4,2,1,3,0:T(8,128)(2,1)S(1)} %bitcast.90), channel_id=1, replica_groups=mesh['seq'=8,'head'=4] {'seq'}, dimensions={0} | all-to-all | bytes 4718592 | tf_op jit(solution)/shard_map/all_to_all | solution.py:136
  898.2 25.3 %all-to-all-done.7 = bf16[8,4,48,1,768]{4,2,0,3,1:T(8,128)(2,1)S(1)} async-done(((bf16[8,4,48,1,768]{4,2,0,3,1:T(8,128)(2,1)}), bf16[8,4,48,1,768]{4,2,0,3,1:T(8,128)(2,1)S(1)}, u32[]{:S(2)}, u32[]{:S(2)}) %all-to-all-start.7) | async-done | bytes 2359328 | tf_op jit(solution)/shard_map/all_to_all | solution.py:135
  927.2 8.9 gather_fusion.9
  (126 shorter events, 141.6 us)
Async XLA Ops:
  0.0 26.9 %copy-start = (bf16[384,3072]{1,0:T(8,128)(2,1)S(1)}, bf16[384,3072]{1,0:T(8,128)(2,1)}, u32[]{:S(2)}) copy-start(bf16[384,3072]{1,0:T(8,128)(2,1)} %param.8) | copy-start | bytes 7077892
  4.6 0.6 copy-start.5
  23.6 13.1 %all-to-all-start.3 = ((s32[8,144,4]{1,0,2:T(8,128)}), s32[8,144,4]{1,0,2:T(8,128)S(1)}, u32[]{:S(2)}, u32[]{:S(2)}) async-start(s32[8,144,4]{1,0,2:T(8,128)} %copy.80), calls=%async_computation.3 | async-start | bytes 65536 | tf_op jit(solution)/shard_map/all_to_all | solution.py:70
  36.8 58.5 %all-to-all-start.4 = ((bf16[8,48,4,768]{3,1,2,0:T(8,128)(2,1)}), bf16[8,48,4,768]{3,1,2,0:T(8,128)(2,1)S(1)}, u32[]{:S(2)}, u32[]{:S(2)}) async-start(bf16[8,48,4,768]{3,1,2,0:T(8,128)(2,1)} %copy.83), calls=%async_computation.4 | async-start | bytes 4718592 | tf_op jit(solution)/shard_map/all_to_all | solution.py:57
  78.2 3.8 copy-start.3
  95.2 312.2 %all-to-all-start = ((bf16[8,144,4,1536]{3,1,2,0:T(8,128)(2,1)}), bf16[8,144,4,1536]{3,1,2,0:T(8,128)(2,1)}, u32[]{:S(2)}, u32[]{:S(2)}) async-start(bf16[8,144,4,1536]{3,1,2,0:T(8,128)(2,1)} %copy.77), calls=%async_computation | async-start | bytes 28311552 | tf_op jit(solution)/shard_map/all_to_all | solution.py:64
  407.4 33.0 %all-to-all-start.5 = ((bf16[8,48,4,768]{3,1,0,2:T(8,128)(2,1)}), bf16[8,48,4,768]{3,1,0,2:T(8,128)(2,1)}, u32[]{:S(2)}, u32[]{:S(2)}) async-start(bf16[8,48,4,768]{3,1,0,2:T(8,128)(2,1)} %copy.84), calls=%async_computation.5 | async-start | bytes 4718592 | tf_op jit(solution)/shard_map/all_to_all | solution.py:56
  422.4 24.6 %copy-start.2 = (s32[32]{0:T(128)S(1)}, s32[32]{0:T(128)}, u32[]{:S(2)}) copy-start(s32[32]{0:T(128)} %param.13) | copy-start | bytes 388
  422.4 25.4 %copy-start.6 = (s32[4,4]{1,0:T(4,128)S(1)}, s32[4,4]{1,0:T(4,128)}, u32[]{:S(2)}) copy-start(s32[4,4]{1,0:T(4,128)} %param.12) | copy-start | bytes 196
  440.4 161.5 %all-to-all-start.1 = ((bf16[8,144,4,1536]{3,1,0,2:T(8,128)(2,1)}), bf16[8,144,4,1536]{3,1,0,2:T(8,128)(2,1)}, u32[]{:S(2)}, u32[]{:S(2)}) async-start(bf16[8,144,4,1536]{3,1,0,2:T(8,128)(2,1)} %copy.78), calls=%async_computation.1 | async-start | bytes 28311552 | tf_op jit(solution)/shard_map/all_to_all | solution.py:63
  669.7 154.8 %copy-start.4 = (s32[2048]{0:T(1024)S(1)}, s32[2048]{0:T(1024)}, u32[]{:S(2)}) copy-start(s32[2048]{0:T(1024)} %pad_clamp_fusion.2) | copy-start | bytes 24580
  891.2 32.3 %all-to-all-start.7 = ((bf16[8,4,48,1,768]{4,2,0,3,1:T(8,128)(2,1)}), bf16[8,4,48,1,768]{4,2,0,3,1:T(8,128)(2,1)S(1)}, u32[]{:S(2)}, u32[]{:S(2)}) async-start(bf16[8,4,48,1,768]{4,2,0,3,1:T(8,128)(2,1)} %copy.92), calls=%async_computation.7 | async-start | bytes 4718592 | tf_op jit(solution)/shard_map/all_to_all | solution.py:135
  927.2 8.9 copy-start.1
where the time goes:
time: 942 us; the launch traced here: 936 us
  waiting for transfers between devices  462 us (49%)
  local copies, waits for them, and re-layouts  270 us (29%)
  blocking collectives  70.9 us (8%)
  matrix products  60.1 us (6%)
  other arithmetic  45.6 us (5%)
  starting transfers between devices  27.4 us (3%)
    all_to_all x1, waiting for transfers between devices, body(): lax.all_to_all(wide_pair, 'seq', split_axis=0, concat_axis=0, tiled=True)  305 us
    all_to_all x1, waiting for transfers between devices, body(): lax.all_to_all(lax.all_to_all(wide_pair, 'seq', split_axis=0, concat_axis...  112 us
    all_to_all x1, blocking collectives, body(): lax.all_to_all(outgoing, 'seq', split_axis=0, concat_axis=0, tiled=True)  57.1 us
    gather x4, local copies, waits for them, and re-layouts, one_tile(): picked = pair_blocks[windows]  37.8 us
    dot_general x4, matrix products, one_tile(): jnp.einsum('qhd,khd->hqk', query_blk, keys_blk, preferred_element_type=jn...  32.3 us
    reduce_sum x4, other arithmetic, one_tile(): total = jnp.sum(weights, axis=2)  31.6 us
    gather x1, local copies, waits for them, and re-layouts, body(): pair_ext = padded[place_ext]  30.7 us
    dot_general x4, matrix products, one_tile(): jnp.einsum('hqk,khd->qhd', weights.astype(jnp.bfloat16), values_blk, pref...  27.8 us
  transfers between devices with their start and end apart: 6, of which 5 were waited for; matrix products, arithmetic and copies ran while one was open for 13% of the time, Pallas kernels for 0%

commit v1 on v0

v1 whole, which is shorter than its diff:
```python
import functools

import jax
import jax.numpy as jnp
from jax import lax
from jax.experimental import pallas as pl
from jax.experimental.pallas import tpu as pltpu
from jax.sharding import PartitionSpec as P

HEAD_DIM = 128


def attn_kernel(win, tile, scale, win_ref, vcw_ref, vco_ref, q_ref, *refs):
    k_refs = refs[:win]
    v_refs = refs[win : 2 * win]
    o_ref = refs[2 * win]
    s_scr = refs[2 * win + 1]
    i = pl.program_id(0)
    q = q_ref[...]
    col = lax.broadcasted_iota(jnp.int32, (tile, tile), 1)
    for w in range(win):
        s = lax.dot_general(
            q, k_refs[w][...], (((1,), (1,)), ((), ())), preferred_element_type=jnp.float32
        )
        s = s * scale
        s = jnp.where(col < vcw_ref[i * win + w], s, -jnp.inf)
        s_scr[:, w * tile : (w + 1) * tile] = s
    s = s_scr[...]
    m = jnp.max(s, axis=1, keepdims=True)
    p = jnp.exp(s - m)
    total = jnp.sum(p, axis=1, keepdims=True)
    pb = p.astype(jnp.bfloat16)
    acc = jnp.dot(pb[:, 0:tile], v_refs[0][...], preferred_element_type=jnp.float32)
    for w in range(1, win):
        acc = acc + jnp.dot(
            pb[:, w * tile : (w + 1) * tile], v_refs[w][...], preferred_element_type=jnp.float32
        )
    out = acc / total
    row = lax.broadcasted_iota(jnp.int32, (tile, 1), 0)
    out = jnp.where(row < vco_ref[i], out, 0.0)
    o_ref[...] = out.astype(o_ref.dtype)


def attention(q_tile, kv_ext, win_flat, vcw_flat, vc_own, tile, win, heads_here):
    tok_dev, pw = q_tile.shape
    tile_dev = tok_dev // tile
    scale = HEAD_DIM ** (-0.5)

    def q_map(i, j, w_ref, a_ref, b_ref):
        return (i, j)

    def k_map(w, i, j, w_ref, a_ref, b_ref):
        return (w_ref[i * win + w], j)

    def v_map(w, i, j, w_ref, a_ref, b_ref):
        return (w_ref[i * win + w], heads_here + j)

    blk = (tile, HEAD_DIM)
    in_specs = [pl.BlockSpec(blk, q_map)]
    in_specs += [pl.BlockSpec(blk, functools.partial(k_map, w)) for w in range(win)]
    in_specs += [pl.BlockSpec(blk, functools.partial(v_map, w)) for w in range(win)]
    steps = tile_dev * heads_here
    cost = pl.CostEstimate(
        flops=steps * 4 * tile * win * tile * HEAD_DIM,
        transcendentals=steps * tile * win * tile,
        bytes_accessed=steps * (2 * win + 2) * tile * HEAD_DIM * 2,
    )
    return pl.pallas_call(
        functools.partial(attn_kernel, win, tile, scale),
        out_shape=jax.ShapeDtypeStruct((tok_dev, pw), jnp.bfloat16),
        grid_spec=pltpu.PrefetchScalarGridSpec(
            num_scalar_prefetch=3,
            grid=(tile_dev, heads_here),
            in_specs=in_specs,
            out_specs=pl.BlockSpec(blk, q_map),
            scratch_shapes=[pltpu.VMEM((tile, win * tile), jnp.float32)],
        ),
        cost_estimate=cost,
    )(win_flat, vcw_flat, vc_own, q_tile, *([kv_ext] * (2 * win)))


def body(query, key, value, raster_to_tile, window_list, valid_count):
    seq_count = lax.axis_size("seq")
    head_count = lax.axis_size("head")
    seq_pos = lax.axis_index("seq")
    rows_here, width = query.shape
    part_width = width // head_count
    tile_dev, win = window_list.shape
    tok_dev = rows_here * head_count
    tile = tok_dev // tile_dev
    share = rows_here // seq_count
    reach = win - 1
    rim = reach * tile
    ext_tiles = tile_dev + 2 * reach
    heads_here = part_width // HEAD_DIM
    all_tiles = valid_count.shape[0]

    order = jnp.argsort(raster_to_tile)
    slots_sorted = raster_to_tile[order].reshape(seq_count, share)
    joined = jnp.concatenate(
        [
            query.reshape(rows_here, head_count, part_width),
            key.reshape(rows_here, head_count, part_width),
            value.reshape(rows_here, head_count, part_width),
        ],
        axis=2,
    )
    joined_sorted = joined[order].reshape(seq_count, share, head_count, 3 * part_width)
    slot_send = jnp.broadcast_to(slots_sorted[:, :, None], (seq_count, share, head_count))

    def exchange(x):
        x = lax.all_to_all(x, "seq", split_axis=0, concat_axis=0, tiled=True)
        return lax.all_to_all(x, "head", split_axis=2, concat_axis=1, tiled=True)

    joined_in = exchange(joined_sorted).reshape(tok_dev, 3 * part_width)
    slot_in = exchange(slot_send).reshape(tok_dev)
    local = slot_in - seq_pos * tok_dev
    place = jnp.zeros((tok_dev,), jnp.int32).at[local].set(jnp.arange(tok_dev, dtype=jnp.int32))
    joined_tile = joined_in[place]
    q_tile = joined_tile[:, :part_width]
    kv_tile = joined_tile[:, part_width:]

    to_right = [(i, i + 1) for i in range(seq_count - 1)]
    to_left = [(i + 1, i) for i in range(seq_count - 1)]
    from_left = lax.ppermute(kv_tile[tok_dev - rim :], "seq", to_right)
    from_right = lax.ppermute(kv_tile[:rim], "seq", to_left)
    kv_ext = jnp.concatenate([from_left, kv_tile, from_right], axis=0)

    first_tile = seq_pos * tile_dev - reach
    global_tiles = jnp.clip(first_tile + jnp.arange(ext_tiles, dtype=jnp.int32), 0, all_tiles - 1)
    vc_ext = valid_count[global_tiles]
    local_windows = (window_list - first_tile).astype(jnp.int32)
    win_flat = local_windows.reshape(tile_dev * win)
    vcw_flat = vc_ext[local_windows].reshape(tile_dev * win)
    vc_own = vc_ext[reach : reach + tile_dev]

    out_tile = attention(q_tile, kv_ext, win_flat, vcw_flat, vc_own, tile, win, heads_here)

    outgoing = out_tile[local].reshape(seq_count, head_count, share, 1, part_width)
    arrived = lax.all_to_all(
        lax.all_to_all(outgoing, "seq", split_axis=0, concat_axis=0, tiled=True),
        "head",
        split_axis=1,
        concat_axis=3,
        tiled=True,
    )
    sorted_rows = arrived.reshape(rows_here, width)
    inverse = (
        jnp.zeros((rows_here,), jnp.int32).at[order].set(jnp.arange(rows_here, dtype=jnp.int32))
    )
    return sorted_rows[inverse]


def solution(mesh):
    placed = (
        P(("seq", "head"), None),
        P(("seq", "head"), None),
        P(("seq", "head"), None),
        P(("seq", "head")),
        P("seq", None),
        P(),
    )
    return jax.shard_map(
        body, mesh=mesh, in_specs=placed, out_specs=P(("seq", "head"), None), check_vma=False
    )
```

time: 942 us -> 658 us (0.70)
  local copies, waits for them, and re-layouts: 270 us -> 115 us
  waiting for transfers between devices: 462 us -> 391 us
  matrix products: 60.1 us -> 0 us
  Pallas kernels: 0 us -> 38 us
  other arithmetic: 45.6 us -> 21.6 us
  blocking collectives: 70.9 us -> 57.5 us
    all_to_all x5 -> x4, waiting for transfers between devices: 436 us -> 225 us  [the longest x2 153 us: exchange(): x = lax.all_to_all(x, 'seq', split_axis=0, concat_axis=0, tiled=True)]
    ppermute x0 -> x2, waiting for transfers between devices: none -> 141 us  [the longest x1 75.6 us: body(): from_left = lax.ppermute(kv_tile[tok_dev - rim:], 'seq', to_right)]
    gather x14 -> x4, local copies, waits for them, and re-layouts: 104 us -> 37.9 us  [the longest x1 18.1 us: body(): joined_tile = joined_in[place]]
    dot_general x8 -> x0, matrix products: 60.1 us -> none  [the longest x4 32.3 us: one_tile(): jnp.einsum('qhd,khd->hqk', query_blk, keys_blk, preferred_element_type=jn...]
    pallas_call x0 -> x1, Pallas kernels: none -> 38 us  [attention(): pl.pallas_call(functools.partial(attn_kernel, win, tile, scale), out_shap...]
    reduce_sum x4 -> x0, other arithmetic: 31.6 us -> none  [one_tile(): total = jnp.sum(weights, axis=2)]
    reshape x6 -> x3, local copies, waits for them, and re-layouts: 36.7 us -> 13.1 us  [the longest x1 6.99 us: body(): joined[order].reshape(seq_count, share, head_count, 3 * part_width)]
    scatter x1 -> x0, local copies, waits for them, and re-layouts: 17.4 us -> none  [body(): place_ext = jnp.full((ext_rows,), 3 * tok_dev, jnp.int32).at[target].set(...]
  transfers between devices with their start and end apart: 6 -> 7, of which waited for: 5 -> 5; matrix products, arithmetic and copies ran while one was open for 13% -> 11% of each run, Pallas kernels for 0% -> 0%
where the time goes in v1:
time: 658 us; the launch traced here: 656 us
  waiting for transfers between devices  391 us (59%)
  local copies, waits for them, and re-layouts  115 us (17%)
  blocking collectives  57.5 us (9%)
  Pallas kernels  38 us (6%)
  starting transfers between devices  33.4 us (5%)
  other arithmetic  21.6 us (3%)
    all_to_all x2, waiting for transfers between devices, exchange(): x = lax.all_to_all(x, 'seq', split_axis=0, concat_axis=0, tiled=True)  153 us
    ppermute x1, waiting for transfers between devices, body(): from_left = lax.ppermute(kv_tile[tok_dev - rim:], 'seq', to_right)  75.6 us
    all_to_all x2, waiting for transfers between devices, exchange(): return lax.all_to_all(x, 'head', split_axis=2, concat_axis=1, tiled=True)  72 us
    ppermute x1, waiting for transfers between devices, body(): from_right = lax.ppermute(kv_tile[:rim], 'seq', to_left)  65.4 us
    all_to_all x1, blocking collectives, body(): lax.all_to_all(outgoing, 'seq', split_axis=0, concat_axis=0, tiled=True)  57.5 us
    pallas_call x1, Pallas kernels, attention(): pl.pallas_call(functools.partial(attn_kernel, win, tile, scale), out_shap...  38 us
    all_to_all x1, waiting for transfers between devices, body(): lax.all_to_all(lax.all_to_all(outgoing, 'seq', split_axis=0, concat_axis=...  25.1 us
    gather x1, local copies, waits for them, and re-layouts, body(): joined_tile = joined_in[place]  18.1 us
  transfers between devices with their start and end apart: 7, of which 5 were waited for; matrix products, arithmetic and copies ran while one was open for 11% of the time, Pallas kernels for 0%

profile of v1, /device:TPU:0, one launch (start us, length us, event | category | flops | bytes accessed | tf_op | source)
XLA Modules:
  0.0 656.3 jit_solution(7190250077362527738)
XLA Ops:
  0.0 4.5 sort.17
  5.1 3.6 gather_fusion.3
  9.5 7.3 %all-to-all-start.2 = ((s32[8,1,192]{2,1,0:T(1,128)}), s32[8,1,192]{2,1,0:T(1,128)S(1)}, u32[]{:S(2)}, u32[]{:S(2)}) async-start(s32[8,1,192]{2,1,0:T(1,128)} %reshape.168), calls=%async_computation.2 | async-start | bytes 16384 | tf_op jit(solution)/shard_map/all_to_all | solution.py:112
  16.8 4.5 reshape.78
  21.3 5.5 reshape.77
  26.9 5.5 reshape.76
  32.4 6.6 %pad_maximum_fusion.1 = bf16[384,4,2304]{2,1,0:T(4,128)(2,1)} fusion(bf16[384,4,768]{2,1,0:T(4,128)(2,1)S(1)} %reshape.78, bf16[384,4,768]{2,1,0:T(4,128)(2,1)} %reshape.77, bf16[384,4,768]{2,1,0:T(4,128)(2,1)} %reshape.76), kind=kLoop, calls=%fused_computation.10 | loop fusion | flops 21233664 | bytes 14155776 | tf_op jit(solution)/shard_map/concatenate | solution.py:100
  39.0 18.0 %gather_fusion.2 = bf16[384,4,2304]{2,1,0:T(4,128)(2,1)} fusion(bf16[384,4,2304]{2,1,0:T(4,128)(2,1)} %pad_maximum_fusion.1, s32[1024]{0:T(1024)S(1)} %pad_clamp_fusion.3), kind=kCustom, calls=%fused_computation.2 | custom fusion | bytes 14157312 | tf_op jit(solution)/shard_map/gather | solution.py:108
  57.0 7.0 %copy.20 = bf16[8,48,4,2304]{3,1,2,0:T(8,128)(2,1)} copy(bf16[8,48,4,2304]{3,2,1,0:T(4,128)(2,1)} %bitcast.33) | data formatting | bytes 14155776 | tf_op jit(solution)/shard_map/reshape | solution.py:108
  64.0 6.0 all-to-all-start
  71.9 152.6 %all-to-all-done = bf16[8,48,4,2304]{3,1,2,0:T(8,128)(2,1)} async-done(((bf16[8,48,4,2304]{3,1,2,0:T(8,128)(2,1)}), bf16[8,48,4,2304]{3,1,2,0:T(8,128)(2,1)}, u32[]{:S(2)}, u32[]{:S(2)}) %all-to-all-start) | async-done | bytes 7077920 | tf_op jit(solution)/shard_map/all_to_all | solution.py:112
  224.5 3.2 all-to-all-start.3
  227.8 6.4 copy.21
  234.2 5.6 all-to-all-start.1
  240.7 6.2 scatter_custom_fusion
  246.9 71.9 %all-to-all-done.1 = bf16[8,48,4,2304]{3,1,0,2:T(8,128)(2,1)} async-done(((bf16[8,48,4,2304]{3,1,0,2:T(8,128)(2,1)}), bf16[8,48,4,2304]{3,1,0,2:T(8,128)(2,1)}, u32[]{:S(2)}, u32[]{:S(2)}) %all-to-all-start.1) | async-done | bytes 7077920 | tf_op jit(solution)/shard_map/all_to_all | solution.py:113
  318.8 6.6 %copy.22 = bf16[8,4,48,1,2304]{4,2,1,0,3:T(8,128)(2,1)} copy(bf16[8,4,48,1,2304]{4,2,0,1,3:T(8,128)(2,1)} %bitcast.3) | data formatting | bytes 14155776 | tf_op jit(solution)/shard_map/all_to_all | solution.py:113
  325.4 18.1 %gather_fusion.4 = bf16[1536,2304]{1,0:T(8,128)(2,1)} fusion(bf16[1536,2304]{1,0:T(8,128)(2,1)} %bitcast.31, s32[2048]{0:T(1024)S(1)} %pad_clamp_fusion.1), kind=kCustom, calls=%fused_computation.4 | custom fusion | bytes 14161920 | tf_op jit(solution)/shard_map/gather | solution.py:119
  343.5 5.4 fusion.6
  350.2 6.3 collective-permute-start
  360.3 3.4 slice.36.q_ref
  363.7 65.4 %collective-permute-done.1 = bf16[1152,1536]{1,0:T(8,128)(2,1)} collective-permute-done((bf16[1152,1536]{1,0:T(8,128)(2,1)}, bf16[1152,1536]{1,0:T(8,128)(2,1)}, u32[]{:S(2)}, u32[]{:S(2)}) %collective-permute-start.1) | collective-permute-done | bytes 3538976 | tf_op jit(solution)/shard_map/ppermute | solution.py:126
  429.1 75.6 %collective-permute-done = bf16[1152,1536]{1,0:T(8,128)(2,1)} collective-permute-done((bf16[1152,1536]{1,0:T(8,128)(2,1)S(1)}, bf16[1152,1536]{1,0:T(8,128)(2,1)}, u32[]{:S(2)}, u32[]{:S(2)}) %collective-permute-start) | collective-permute-done | bytes 3538976 | tf_op jit(solution)/shard_map/ppermute | solution.py:125
  504.7 8.5 %pad_maximum_fusion.refs_0_.refs_1_.refs_2_.refs_3_.refs_4_.refs_5_.refs_6_.refs_7_ = bf16[3840,1536]{1,0:T(8,128)(2,1)} fusion(bf16[1152,1536]{1,0:T(8,128)(2,1)} %collective-permute-done.1, bf16[1536,1536]{1,0:T(8,128)(2,1)S(1)} %slice-done, bf16[1152,1536]{1,0:T(8,128)(2,1)} %collective-permute-done), kind=kLoop, calls=%fused_computation.9 | loop fusion | flops 35389440 | bytes 23592960 | tf_op jit(solution)/shard_map/concatenate | solution.py:127
  513.1 38.0 %shard_map.64 = bf16[1536,768]{1,0:T(8,128)(2,1)} custom-call(s32[16]{0:T(128)} %reshape.74.win_ref, s32[16]{0:T(128)} %gather_fusion.1, s32[4]{0:T(128)} %slice.17.vco_ref, bf16[1536,768]{1,0:T(8,128)(2,1)} %slice.36.q_ref, bf16[3840,1536]{1,0:T(8,128)(2,1)} %pad_maximum_fusion.refs_0_.refs_1_.refs_2_.refs_3_.refs_4_.refs_5_.refs_6_.refs_7_, ...), custom_call_target="tpu_custom_call" | custom-call | flops 7247757312 | bytes 23592960 | tf_op jit(solution)/shard_map/pallas_call | solution.py:68
  551.2 8.1 %gather_fusion.5 = bf16[1536,768]{1,0:T(8,128)(2,1)S(1)} fusion(bf16[1536,768]{1,0:T(8,128)(2,1)} %shard_map.64, s32[2048]{0:T(1024)S(1)} %pad_clamp_fusion), kind=kCustom, calls=%fused_computation.5 | custom fusion | bytes 4724736 | tf_op jit(solution)/shard_map/gather | solution.py:139
  559.2 57.5 %all_to_all.54 = bf16[8,4,48,1,768]{4,2,1,3,0:T(8,128)(2,1)S(1)} all-to-all(bf16[8,4,48,1,768]{4,2,1,3,0:T(8,128)(2,1)S(1)} %bitcast.34), channel_id=1, replica_groups=mesh['seq'=8,'head'=4] {'seq'}, dimensions={0} | all-to-all | bytes 4718592 | tf_op jit(solution)/shard_map/all_to_all | solution.py:141
  618.3 3.6 all-to-all-start.5
  622.0 3.3 scatter_custom_fusion.1
  625.3 25.1 %all-to-all-done.5 = bf16[8,4,48,1,768]{4,2,0,3,1:T(8,128)(2,1)S(1)} async-done(((bf16[8,4,48,1,768]{4,2,0,3,1:T(8,128)(2,1)}), bf16[8,4,48,1,768]{4,2,0,3,1:T(8,128)(2,1)S(1)}, u32[]{:S(2)}, u32[]{:S(2)}) %all-to-all-start.5) | async-done | bytes 2359328 | tf_op jit(solution)/shard_map/all_to_all | solution.py:140
  650.4 1.8 copy.27
  652.7 3.6 gather_fusion.6
  (50 shorter events, 11.4 us)
Async XLA Ops:
  0.0 357.2 %copy-start = (s32[32]{0:T(128)S(1)}, s32[32]{0:T(128)}, u32[]{:S(2)}) copy-start(s32[32]{0:T(128)} %param.11) | copy-start | bytes 388
  4.5 0.6 copy-start.3
  9.5 54.5 %all-to-all-start.2 = ((s32[8,1,192]{2,1,0:T(1,128)}), s32[8,1,192]{2,1,0:T(1,128)S(1)}, u32[]{:S(2)}, u32[]{:S(2)}) async-start(s32[8,1,192]{2,1,0:T(1,128)} %reshape.168), calls=%async_computation.2 | async-start | bytes 16384 | tf_op jit(solution)/shard_map/all_to_all | solution.py:112
  64.0 160.5 %all-to-all-start = ((bf16[8,48,4,2304]{3,1,2,0:T(8,128)(2,1)}), bf16[8,48,4,2304]{3,1,2,0:T(8,128)(2,1)}, u32[]{:S(2)}, u32[]{:S(2)}) async-start(bf16[8,48,4,2304]{3,1,2,0:T(8,128)(2,1)} %copy.20), calls=%async_computation | async-start | bytes 14155776 | tf_op jit(solution)/shard_map/all_to_all | solution.py:112
  224.5 9.7 %all-to-all-start.3 = ((s32[4,1,384]{2,1,0:T(1,128)}), s32[4,1,384]{2,1,0:T(1,128)S(1)}, u32[]{:S(2)}, u32[]{:S(2)}) async-start(s32[4,1,384]{2,1,0:T(1,128)} %reshape.170), calls=%async_computation.3 | async-start | bytes 12288 | tf_op jit(solution)/shard_map/all_to_all | solution.py:113
  234.2 84.7 %all-to-all-start.1 = ((bf16[8,48,4,2304]{3,1,0,2:T(8,128)(2,1)}), bf16[8,48,4,2304]{3,1,0,2:T(8,128)(2,1)}, u32[]{:S(2)}, u32[]{:S(2)}) async-start(bf16[8,48,4,2304]{3,1,0,2:T(8,128)(2,1)} %copy.21), calls=%async_computation.1 | async-start | bytes 14155776 | tf_op jit(solution)/shard_map/all_to_all | solution.py:113
  240.6 6.2 copy-start.2
  343.5 13.0 %copy-start.4 = (s32[4,4]{1,0:T(4,128)S(1)}, s32[4,4]{1,0:T(4,128)}, u32[]{:S(2)}) copy-start(s32[4,4]{1,0:T(4,128)} %param.10) | copy-start | bytes 196
  348.9 80.2 %collective-permute-start.1 = (bf16[1152,1536]{1,0:T(8,128)(2,1)}, bf16[1152,1536]{1,0:T(8,128)(2,1)}, u32[]{:S(2)}, u32[]{:S(2)}) collective-permute-start(bf16[1152,1536]{1,0:T(8,128)(2,1)} %get-tuple-element.10), channel_id=1, source_target_pairs={{4,0},{8,4},{12,8},{16,12},{20,16},{24,20},{28,24},{5,1},{9,5},{13... | collective-permute-start | bytes 10616840 | tf_op jit(solution)/shard_map/ppermute | solution.py:126
  350.2 154.5 %collective-permute-start = (bf16[1152,1536]{1,0:T(8,128)(2,1)S(1)}, bf16[1152,1536]{1,0:T(8,128)(2,1)}, u32[]{:S(2)}, u32[]{:S(2)}) collective-permute-start(bf16[1152,1536]{1,0:T(8,128)(2,1)S(1)} %get-tuple-element.9), channel_id=1, source_target_pairs={{0,4},{4,8},{8,12},{12,16},{16,20},{20,24},{24,28},{1,5},{5,9},{9,... | collective-permute-start | bytes 10616840 | tf_op jit(solution)/shard_map/ppermute | solution.py:125
  360.3 144.3 %slice-start = ((bf16[1536,2304]{1,0:T(8,128)(2,1)}), bf16[1536,1536]{1,0:T(8,128)(2,1)S(1)}, s32[]{:S(2)}) async-start(bf16[1536,2304]{1,0:T(8,128)(2,1)} %gather_fusion.4), calls=%async_computation.6 | async-start | bytes 9437184 | tf_op jit(solution)/shard_map/slice | solution.py:121
  618.3 32.1 %all-to-all-start.5 = ((bf16[8,4,48,1,768]{4,2,0,3,1:T(8,128)(2,1)}), bf16[8,4,48,1,768]{4,2,0,3,1:T(8,128)(2,1)S(1)}, u32[]{:S(2)}, u32[]{:S(2)}) async-start(bf16[8,4,48,1,768]{4,2,0,3,1:T(8,128)(2,1)} %copy.26), calls=%async_computation.5 | async-start | bytes 4718592 | tf_op jit(solution)/shard_map/all_to_all | solution.py:140
  652.7 3.6 copy-start.1

commit v2 on v1

--- a/solution.py
+++ b/solution.py
@@ -109,8 +109,9 @@
     slot_send = jnp.broadcast_to(slots_sorted[:, :, None], (seq_count, share, head_count))
 
     def exchange(x):
-        x = lax.all_to_all(x, "seq", split_axis=0, concat_axis=0, tiled=True)
-        return lax.all_to_all(x, "head", split_axis=2, concat_axis=1, tiled=True)
+        lead = x.shape[1:2]
+        x = jnp.swapaxes(x, 1, 2).reshape((seq_count * head_count,) + lead + x.shape[3:])
+        return lax.all_to_all(x, ("seq", "head"), split_axis=0, concat_axis=0, tiled=True)
 
     joined_in = exchange(joined_sorted).reshape(tok_dev, 3 * part_width)
     slot_in = exchange(slot_send).reshape(tok_dev)
@@ -137,14 +138,10 @@
     out_tile = attention(q_tile, kv_ext, win_flat, vcw_flat, vc_own, tile, win, heads_here)
 
     outgoing = out_tile[local].reshape(seq_count, head_count, share, 1, part_width)
-    arrived = lax.all_to_all(
-        lax.all_to_all(outgoing, "seq", split_axis=0, concat_axis=0, tiled=True),
-        "head",
-        split_axis=1,
-        concat_axis=3,
-        tiled=True,
-    )
-    sorted_rows = arrived.reshape(rows_here, width)
+    outgoing = outgoing.reshape(seq_count * head_count, share, part_width)
+    arrived = lax.all_to_all(outgoing, ("seq", "head"), split_axis=0, concat_axis=0, tiled=True)
+    arrived = arrived.reshape(seq_count, head_count, share, part_width)
+    sorted_rows = jnp.swapaxes(arrived, 1, 2).reshape(rows_here, width)
     inverse = (
         jnp.zeros((rows_here,), jnp.int32).at[order].set(jnp.arange(rows_here, dtype=jnp.int32))
     )

time: 658 us -> 525 us (0.80)
  blocking collectives: 57.5 us -> 0 us
  waiting for transfers between devices: 391 us -> 341 us
  local copies, waits for them, and re-layouts: 115 us -> 98.7 us
  starting transfers between devices: 33.4 us -> 25.4 us
    all_to_all x1 -> x0, blocking collectives: 57.5 us -> none  [body(): lax.all_to_all(outgoing, 'seq', split_axis=0, concat_axis=0, tiled=True)]
    all_to_all x5 -> x3, waiting for transfers between devices: 250 us -> 202 us  [the longest x2 151 us: exchange(): lax.all_to_all(x, ('seq', 'head'), split_axis=0, concat_axis=0, tiled=True)]
    all_to_all x6 -> x0, local copies, waits for them, and re-layouts: 16.9 us -> none  [the longest x3 6.94 us: exchange(): x = lax.all_to_all(x, 'seq', split_axis=0, concat_axis=0, tiled=True)]
    all_to_all x5 -> x3, starting transfers between devices: 25.8 us -> 17.7 us  [the longest x2 13.3 us: exchange(): lax.all_to_all(x, ('seq', 'head'), split_axis=0, concat_axis=0, tiled=True)]
  transfers between devices with their start and end apart: 7 -> 5, of which waited for: 5 -> 4; matrix products, arithmetic and copies ran while one was open for 11% -> 12% of each run, Pallas kernels for 0% -> 0%
where the time goes in v2:
time: 525 us; the launch traced here: 524 us
  waiting for transfers between devices  341 us (65%)
  local copies, waits for them, and re-layouts  98.7 us (19%)
  Pallas kernels  37.8 us (7%)
  starting transfers between devices  25.4 us (5%)
  other arithmetic  20.3 us (4%)
    all_to_all x2, waiting for transfers between devices, exchange(): lax.all_to_all(x, ('seq', 'head'), split_axis=0, concat_axis=0, tiled=True)  151 us
    ppermute x1, waiting for transfers between devices, body(): from_left = lax.ppermute(kv_tile[tok_dev - rim:], 'seq', to_right)  73.9 us
    ppermute x1, waiting for transfers between devices, body(): from_right = lax.ppermute(kv_tile[:rim], 'seq', to_left)  65.5 us
    all_to_all x1, waiting for transfers between devices, body(): lax.all_to_all(outgoing, ('seq', 'head'), split_axis=0, concat_axis=0, ti...  51.3 us
    pallas_call x1, Pallas kernels, attention(): pl.pallas_call(functools.partial(attn_kernel, win, tile, scale), out_shap...  37.8 us
    gather x1, local copies, waits for them, and re-layouts, body(): joined_tile = joined_in[place]  18.1 us
    gather x1, local copies, waits for them, and re-layouts, body(): joined[order].reshape(seq_count, share, head_count, 3 * part_width)  18 us
    all_to_all x2, starting transfers between devices, exchange(): lax.all_to_all(x, ('seq', 'head'), split_axis=0, concat_axis=0, tiled=True)  13.3 us
  transfers between devices with their start and end apart: 5, of which 4 were waited for; matrix products, arithmetic and copies ran while one was open for 12% of the time, Pallas kernels for 0%

profile of v2, /device:TPU:0, one launch (start us, length us, event | category | flops | bytes accessed | tf_op | source)
XLA Modules:
  0.0 523.7 jit_solution(1595614342232358651)
XLA Ops:
  0.0 4.5 sort.17
  5.0 3.6 gather_fusion.3
  8.7 0.6 transpose.11
  9.4 7.3 %all-to-all-start.1 = ((s32[32,1,48]{2,1,0:T(1,128)}), s32[32,1,48]{2,1,0:T(1,128)S(1)}, u32[]{:S(2)}, u32[]{:S(2)}) async-start(s32[32,1,48]{2,1,0:T(1,128)} %bitcast.5), calls=%async_computation.1 | async-start | bytes 32768 | tf_op jit(solution)/shard_map/all_to_all | solution.py:114
  16.7 4.5 reshape.81
  21.2 5.5 %reshape.80 = bf16[384,4,768]{2,1,0:T(4,128)(2,1)} reshape(bf16[384,3072]{1,0:T(8,128)(2,1)} %param.7) | data formatting | bytes 4718592 | tf_op jit(solution)/shard_map/reshape | solution.py:103
  26.8 5.6 %reshape.79 = bf16[384,4,768]{2,1,0:T(4,128)(2,1)} reshape(bf16[384,3072]{1,0:T(8,128)(2,1)} %param.6) | data formatting | bytes 4718592 | tf_op jit(solution)/shard_map/reshape | solution.py:102
  32.3 6.6 %pad_maximum_fusion.1 = bf16[384,4,2304]{2,1,0:T(4,128)(2,1)} fusion(bf16[384,4,768]{2,1,0:T(4,128)(2,1)S(1)} %reshape.81, bf16[384,4,768]{2,1,0:T(4,128)(2,1)} %reshape.80, bf16[384,4,768]{2,1,0:T(4,128)(2,1)} %reshape.79), kind=kLoop, calls=%fused_computation.10 | loop fusion | flops 21233664 | bytes 14155776 | tf_op jit(solution)/shard_map/concatenate | solution.py:100
  38.9 18.0 %gather_fusion.2 = bf16[384,4,2304]{2,1,0:T(4,128)(2,1)} fusion(bf16[384,4,2304]{2,1,0:T(4,128)(2,1)} %pad_maximum_fusion.1, s32[1024]{0:T(1024)S(1)} %pad_clamp_fusion.3), kind=kCustom, calls=%fused_computation.2 | custom fusion | bytes 14157312 | tf_op jit(solution)/shard_map/gather | solution.py:108
  56.9 7.0 %copy.11 = bf16[8,48,4,2304]{3,1,2,0:T(8,128)(2,1)} copy(bf16[8,48,4,2304]{3,2,1,0:T(4,128)(2,1)} %bitcast.16) | data formatting | bytes 14155776 | tf_op jit(solution)/shard_map/reshape | solution.py:108
  63.9 5.9 %all-to-all-start = ((bf16[32,48,2304]{2,1,0:T(8,128)(2,1)}), bf16[32,48,2304]{2,1,0:T(8,128)(2,1)}, u32[]{:S(2)}, u32[]{:S(2)}) async-start(bf16[32,48,2304]{2,1,0:T(8,128)(2,1)} %bitcast.15), calls=%async_computation | async-start | bytes 14155776 | tf_op jit(solution)/shard_map/all_to_all | solution.py:114
  70.1 6.4 %scatter_custom_fusion = s32[1536]{0:T(1024)S(1)} fusion(s32[1536]{0:T(1024)S(1)} %fusion, s32[1536]{0:T(1024)S(1)} %iota.16, s32[]{:T(128)} %constant.14.clone.1), kind=kCustom, calls=%fused_computation.24 | custom fusion | bytes 6148 | tf_op jit(solution)/shard_map/scatter | solution.py:119
  76.5 150.6 %all-to-all-done = bf16[32,48,2304]{2,1,0:T(8,128)(2,1)} async-done(((bf16[32,48,2304]{2,1,0:T(8,128)(2,1)}), bf16[32,48,2304]{2,1,0:T(8,128)(2,1)}, u32[]{:S(2)}, u32[]{:S(2)}) %all-to-all-start) | async-done | bytes 7077920 | tf_op jit(solution)/shard_map/all_to_all | solution.py:114
  227.1 18.1 %gather_fusion.4 = bf16[1536,2304]{1,0:T(8,128)(2,1)} fusion(bf16[1536,2304]{1,0:T(8,128)(2,1)} %bitcast.4, s32[2048]{0:T(1024)S(1)} %pad_clamp_fusion.1), kind=kCustom, calls=%fused_computation.4 | custom fusion | bytes 14161920 | tf_op jit(solution)/shard_map/gather | solution.py:120
  245.2 5.4 %fusion.6 = (bf16[1152,1536]{1,0:T(8,128)(2,1)S(1)}, bf16[1152,1536]{1,0:T(8,128)(2,1)}) fusion(bf16[1536,2304]{1,0:T(8,128)(2,1)} %gather_fusion.4), kind=kLoop, calls=%fused_computation.31 | loop fusion | bytes 14155776 | tf_op jit(solution)/shard_map/slice | solution.py:126
  250.5 1.3 collective-permute-start.1
  251.8 6.3 %collective-permute-start = (bf16[1152,1536]{1,0:T(8,128)(2,1)S(1)}, bf16[1152,1536]{1,0:T(8,128)(2,1)}, u32[]{:S(2)}, u32[]{:S(2)}) collective-permute-start(bf16[1152,1536]{1,0:T(8,128)(2,1)S(1)} %get-tuple-element.9), channel_id=1, source_target_pairs={{0,4},{4,8},{8,12},{12,16},{16,20},{20,24},{24,28},{1,5},{5,9},{9,... | collective-permute-start | bytes 10616840 | tf_op jit(solution)/shard_map/ppermute | solution.py:126
  258.1 0.6 reshape.77.win_ref
  258.9 0.7 gather_fusion
  260.1 1.1 gather_fusion.1
  261.3 0.7 pad_clamp_fusion
  262.0 3.2 slice.36.q_ref
  265.2 65.5 %collective-permute-done.1 = bf16[1152,1536]{1,0:T(8,128)(2,1)} collective-permute-done((bf16[1152,1536]{1,0:T(8,128)(2,1)}, bf16[1152,1536]{1,0:T(8,128)(2,1)}, u32[]{:S(2)}, u32[]{:S(2)}) %collective-permute-start.1) | collective-permute-done | bytes 3538976 | tf_op jit(solution)/shard_map/ppermute | solution.py:127
  330.7 73.9 %collective-permute-done = bf16[1152,1536]{1,0:T(8,128)(2,1)} collective-permute-done((bf16[1152,1536]{1,0:T(8,128)(2,1)S(1)}, bf16[1152,1536]{1,0:T(8,128)(2,1)}, u32[]{:S(2)}, u32[]{:S(2)}) %collective-permute-start) | collective-permute-done | bytes 3538976 | tf_op jit(solution)/shard_map/ppermute | solution.py:126
  404.6 8.4 %pad_maximum_fusion.refs_0_.refs_1_.refs_2_.refs_3_.refs_4_.refs_5_.refs_6_.refs_7_ = bf16[3840,1536]{1,0:T(8,128)(2,1)} fusion(bf16[1152,1536]{1,0:T(8,128)(2,1)} %collective-permute-done.1, bf16[1536,1536]{1,0:T(8,128)(2,1)S(1)} %slice-done, bf16[1152,1536]{1,0:T(8,128)(2,1)} %collective-permute-done), kind=kLoop, calls=%fused_computation.9 | loop fusion | flops 35389440 | bytes 23592960 | tf_op jit(solution)/shard_map/concatenate | solution.py:128
  413.0 37.8 %shard_map.64 = bf16[1536,768]{1,0:T(8,128)(2,1)} custom-call(s32[16]{0:T(128)} %reshape.77.win_ref, s32[16]{0:T(128)} %gather_fusion.1, s32[4]{0:T(128)} %slice.17.vco_ref, bf16[1536,768]{1,0:T(8,128)(2,1)} %slice.36.q_ref, bf16[3840,1536]{1,0:T(8,128)(2,1)} %pad_maximum_fusion.refs_0_.refs_1_.refs_2_.refs_3_.refs_4_.refs_5_.refs_6_.refs_7_, ...), custom_call_target="tpu_custom_call" | custom-call | flops 7247757312 | bytes 23592960 | tf_op jit(solution)/shard_map/pallas_call | solution.py:68
  450.9 8.7 %gather_fusion.5 = bf16[1536,768]{1,0:T(8,128)(2,1)} fusion(bf16[1536,768]{1,0:T(8,128)(2,1)} %shard_map.64, s32[2048]{0:T(1024)S(1)} %pad_clamp_fusion), kind=kCustom, calls=%fused_computation.5 | custom fusion | bytes 4724736 | tf_op jit(solution)/shard_map/gather | solution.py:140
  459.5 4.5 all-to-all-start.2
  464.0 3.0 scatter_custom_fusion.1
  467.1 51.3 %all-to-all-done.2 = bf16[32,48,768]{2,1,0:T(8,128)(2,1)S(1)} async-done(((bf16[32,48,768]{2,1,0:T(8,128)(2,1)}), bf16[32,48,768]{2,1,0:T(8,128)(2,1)S(1)}, u32[]{:S(2)}, u32[]{:S(2)}) %all-to-all-start.2) | async-done | bytes 2359328 | tf_op jit(solution)/shard_map/all_to_all | solution.py:142
  518.4 1.2 copy.12
  520.1 3.6 gather_fusion.6
  (33 shorter events, 2.1 us)
Async XLA Ops:
  0.0 258.9 %copy-start = (s32[32]{0:T(128)S(1)}, s32[32]{0:T(128)}, u32[]{:S(2)}) copy-start(s32[32]{0:T(128)} %param.11) | copy-start | bytes 388
  4.5 0.6 copy-start.3
  9.4 54.6 %all-to-all-start.1 = ((s32[32,1,48]{2,1,0:T(1,128)}), s32[32,1,48]{2,1,0:T(1,128)S(1)}, u32[]{:S(2)}, u32[]{:S(2)}) async-start(s32[32,1,48]{2,1,0:T(1,128)} %bitcast.5), calls=%async_computation.1 | async-start | bytes 32768 | tf_op jit(solution)/shard_map/all_to_all | solution.py:114
  63.9 163.2 %all-to-all-start = ((bf16[32,48,2304]{2,1,0:T(8,128)(2,1)}), bf16[32,48,2304]{2,1,0:T(8,128)(2,1)}, u32[]{:S(2)}, u32[]{:S(2)}) async-start(bf16[32,48,2304]{2,1,0:T(8,128)(2,1)} %bitcast.15), calls=%async_computation | async-start | bytes 14155776 | tf_op jit(solution)/shard_map/all_to_all | solution.py:114
  70.1 6.4 %copy-start.2 = (s32[1536]{0:T(1024)}, s32[1536]{0:T(1024)S(1)}, u32[]{:S(2)}) copy-start(s32[1536]{0:T(1024)S(1)} %fusion) | copy-start | bytes 18436
  245.2 13.0 %copy-start.4 = (s32[4,4]{1,0:T(4,128)S(1)}, s32[4,4]{1,0:T(4,128)}, u32[]{:S(2)}) copy-start(s32[4,4]{1,0:T(4,128)} %param.10) | copy-start | bytes 196
  250.5 80.2 %collective-permute-start.1 = (bf16[1152,1536]{1,0:T(8,128)(2,1)}, bf16[1152,1536]{1,0:T(8,128)(2,1)}, u32[]{:S(2)}, u32[]{:S(2)}) collective-permute-start(bf16[1152,1536]{1,0:T(8,128)(2,1)} %get-tuple-element.10), channel_id=1, source_target_pairs={{4,0},{8,4},{12,8},{16,12},{20,16},{24,20},{28,24},{5,1},{9,5},{13... | collective-permute-start | bytes 10616840 | tf_op jit(solution)/shard_map/ppermute | solution.py:127
  251.8 152.8 %collective-permute-start = (bf16[1152,1536]{1,0:T(8,128)(2,1)S(1)}, bf16[1152,1536]{1,0:T(8,128)(2,1)}, u32[]{:S(2)}, u32[]{:S(2)}) collective-permute-start(bf16[1152,1536]{1,0:T(8,128)(2,1)S(1)} %get-tuple-element.9), channel_id=1, source_target_pairs={{0,4},{4,8},{8,12},{12,16},{16,20},{20,24},{24,28},{1,5},{5,9},{9,... | collective-permute-start | bytes 10616840 | tf_op jit(solution)/shard_map/ppermute | solution.py:126
  265.2 139.4 %slice-start = ((bf16[1536,2304]{1,0:T(8,128)(2,1)}), bf16[1536,1536]{1,0:T(8,128)(2,1)S(1)}, s32[]{:S(2)}) async-start(bf16[1536,2304]{1,0:T(8,128)(2,1)} %gather_fusion.4), calls=%async_computation.3 | async-start | bytes 9437184 | tf_op jit(solution)/shard_map/slice | solution.py:122
  459.5 58.9 %all-to-all-start.2 = ((bf16[32,48,768]{2,1,0:T(8,128)(2,1)}), bf16[32,48,768]{2,1,0:T(8,128)(2,1)S(1)}, u32[]{:S(2)}, u32[]{:S(2)}) async-start(bf16[32,48,768]{2,1,0:T(8,128)(2,1)} %bitcast.6), calls=%async_computation.2 | async-start | bytes 4718592 | tf_op jit(solution)/shard_map/all_to_all | solution.py:142
  520.1 3.6 copy-start.1

commit v3 on v2

--- a/solution.py
+++ b/solution.py
@@ -79,7 +79,7 @@
     )(win_flat, vcw_flat, vc_own, q_tile, *([kv_ext] * (2 * win)))
 
 
-def body(query, key, value, raster_to_tile, window_list, valid_count):
+def body(pos_of_owner, query, key, value, raster_to_tile, window_list, valid_count):
     seq_count = lax.axis_size("seq")
     head_count = lax.axis_size("head")
     seq_pos = lax.axis_index("seq")
@@ -95,8 +95,12 @@
     heads_here = part_width // HEAD_DIM
     all_tiles = valid_count.shape[0]
 
+    owner_at = [0] * seq_count
+    for o, d in enumerate(pos_of_owner):
+        owner_at[d] = o
     order = jnp.argsort(raster_to_tile)
-    slots_sorted = raster_to_tile[order].reshape(seq_count, share)
+    send_order = order.reshape(seq_count, share)[jnp.array(owner_at, jnp.int32)].reshape(rows_here)
+    slots_sorted = raster_to_tile[send_order].reshape(seq_count, share)
     joined = jnp.concatenate(
         [
             query.reshape(rows_here, head_count, part_width),
@@ -105,7 +109,7 @@
         ],
         axis=2,
     )
-    joined_sorted = joined[order].reshape(seq_count, share, head_count, 3 * part_width)
+    joined_sorted = joined[send_order].reshape(seq_count, share, head_count, 3 * part_width)
     slot_send = jnp.broadcast_to(slots_sorted[:, :, None], (seq_count, share, head_count))
 
     def exchange(x):
@@ -115,22 +119,26 @@
 
     joined_in = exchange(joined_sorted).reshape(tok_dev, 3 * part_width)
     slot_in = exchange(slot_send).reshape(tok_dev)
-    local = slot_in - seq_pos * tok_dev
+    my_owner = jnp.array(owner_at, jnp.int32)[seq_pos]
+    local = slot_in - my_owner * tok_dev
     place = jnp.zeros((tok_dev,), jnp.int32).at[local].set(jnp.arange(tok_dev, dtype=jnp.int32))
     joined_tile = joined_in[place]
     q_tile = joined_tile[:, :part_width]
     kv_tile = joined_tile[:, part_width:]
 
-    to_right = [(i, i + 1) for i in range(seq_count - 1)]
-    to_left = [(i + 1, i) for i in range(seq_count - 1)]
+    to_right = [(pos_of_owner[o], pos_of_owner[o + 1]) for o in range(seq_count - 1)]
+    to_left = [(pos_of_owner[o + 1], pos_of_owner[o]) for o in range(seq_count - 1)]
     from_left = lax.ppermute(kv_tile[tok_dev - rim :], "seq", to_right)
     from_right = lax.ppermute(kv_tile[:rim], "seq", to_left)
     kv_ext = jnp.concatenate([from_left, kv_tile, from_right], axis=0)
 
-    first_tile = seq_pos * tile_dev - reach
+    window_mine = lax.ppermute(
+        window_list, "seq", [(o, pos_of_owner[o]) for o in range(seq_count)]
+    )
+    first_tile = my_owner * tile_dev - reach
     global_tiles = jnp.clip(first_tile + jnp.arange(ext_tiles, dtype=jnp.int32), 0, all_tiles - 1)
     vc_ext = valid_count[global_tiles]
-    local_windows = (window_list - first_tile).astype(jnp.int32)
+    local_windows = (window_mine - first_tile).astype(jnp.int32)
     win_flat = local_windows.reshape(tile_dev * win)
     vcw_flat = vc_ext[local_windows].reshape(tile_dev * win)
     vc_own = vc_ext[reach : reach + tile_dev]
@@ -143,9 +151,25 @@
     arrived = arrived.reshape(seq_count, head_count, share, part_width)
     sorted_rows = jnp.swapaxes(arrived, 1, 2).reshape(rows_here, width)
     inverse = (
-        jnp.zeros((rows_here,), jnp.int32).at[order].set(jnp.arange(rows_here, dtype=jnp.int32))
+        jnp.zeros((rows_here,), jnp.int32).at[send_order].set(jnp.arange(rows_here, dtype=jnp.int32))
     )
     return sorted_rows[inverse]
+
+
+def snake(mesh):
+    seq_count = mesh.shape["seq"]
+    first = mesh.devices.reshape(seq_count, -1)[:, 0]
+    try:
+        spots = [tuple(d.coords) for d in first]
+    except AttributeError:
+        spots = [(0, d % 2, d // 2) for d in range(seq_count)]
+    low_z = min(c[2] for c in spots)
+
+    def rank(d):
+        x, y, z = spots[d][:3]
+        return (z, y if (z - low_z) % 2 == 0 else -y, x)
+
+    return tuple(sorted(range(seq_count), key=rank))
 
 
 def solution(mesh):
@@ -158,5 +182,5 @@
         P(),
     )
     return jax.shard_map(
-        body, mesh=mesh, in_specs=placed, out_specs=P(("seq", "head"), None), check_vma=False
+        functools.partial(body, snake(mesh)), mesh=mesh, in_specs=placed, out_specs=P(("seq", "head"), None), check_vma=False
     )

time: 525 us -> 463 us (0.88)
  waiting for transfers between devices: 341 us -> 265 us
  starting transfers between devices: 25.4 us -> 36.4 us
    ppermute x1, waiting for transfers between devices: 73.9 us -> 0.87 us  [body(): from_left = lax.ppermute(kv_tile[tok_dev - rim:], 'seq', to_right)]
    all_to_all x1, starting transfers between devices: 4.47 us -> 14.1 us  [body(): lax.all_to_all(outgoing, ('seq', 'head'), split_axis=0, concat_axis=0, ti...]
    gather x2 -> x3, local copies, waits for them, and re-layouts: 21.6 us -> 22.2 us  [the longest x1 18 us: body(): joined[send_order].reshape(seq_count, share, head_count, 3 * part_width)]
  transfers between devices with their start and end apart: 5 -> 6, of which waited for: 4 -> 4; matrix products, arithmetic and copies ran while one was open for 12% -> 14% of each run, Pallas kernels for 0% -> 0%
where the time goes in v3:
time: 463 us; the launch traced here: 462 us
  waiting for transfers between devices  265 us (57%)
  local copies, waits for them, and re-layouts  100 us (22%)
  Pallas kernels  37.8 us (8%)
  starting transfers between devices  36.4 us (8%)
  other arithmetic  21 us (5%)
    all_to_all x2, waiting for transfers between devices, exchange(): lax.all_to_all(x, ('seq', 'head'), split_axis=0, concat_axis=0, tiled=True)  149 us
    ppermute x1, waiting for transfers between devices, body(): from_right = lax.ppermute(kv_tile[:rim], 'seq', to_left)  63.5 us
    all_to_all x1, waiting for transfers between devices, body(): lax.all_to_all(outgoing, ('seq', 'head'), split_axis=0, concat_axis=0, ti...  51.3 us
    pallas_call x1, Pallas kernels, attention(): pl.pallas_call(functools.partial(attn_kernel, win, tile, scale), out_shap...  37.8 us
    gather x1, local copies, waits for them, and re-layouts, body(): joined_tile = joined_in[place]  18.1 us
    gather x1, local copies, waits for them, and re-layouts, body(): joined[send_order].reshape(seq_count, share, head_count, 3 * part_width)  18 us
    all_to_all x1, starting transfers between devices, body(): lax.all_to_all(outgoing, ('seq', 'head'), split_axis=0, concat_axis=0, ti...  14.1 us
    all_to_all x2, starting transfers between devices, exchange(): lax.all_to_all(x, ('seq', 'head'), split_axis=0, concat_axis=0, tiled=True)  13.3 us
  transfers between devices with their start and end apart: 6, of which 4 were waited for; matrix products, arithmetic and copies ran while one was open for 14% of the time, Pallas kernels for 0%

profile of v3, /device:TPU:0, one launch (start us, length us, event | category | flops | bytes accessed | tf_op | source)
XLA Modules:
  0.0 461.7 jit_solution(7461444162942561229)
XLA Ops:
  0.0 4.5 sort.17
  4.5 0.7 pad_clamp_fusion.4
  6.4 3.6 gather_fusion.4
  10.8 7.3 %all-to-all-start.1 = ((s32[32,1,48]{2,1,0:T(1,128)}), s32[32,1,48]{2,1,0:T(1,128)S(1)}, u32[]{:S(2)}, u32[]{:S(2)}) async-start(s32[32,1,48]{2,1,0:T(1,128)} %bitcast.6), calls=%async_computation.1 | async-start | bytes 32768 | tf_op jit(solution)/shard_map/all_to_all | solution.py:118
  18.1 4.5 reshape.121
  22.6 5.5 %reshape.120 = bf16[384,4,768]{2,1,0:T(4,128)(2,1)} reshape(bf16[384,3072]{1,0:T(8,128)(2,1)} %param.9) | data formatting | bytes 4718592 | tf_op jit(solution)/shard_map/reshape | solution.py:107
  28.2 5.6 %reshape.119 = bf16[384,4,768]{2,1,0:T(4,128)(2,1)} reshape(bf16[384,3072]{1,0:T(8,128)(2,1)} %param.8) | data formatting | bytes 4718592 | tf_op jit(solution)/shard_map/reshape | solution.py:106
  33.7 6.6 %pad_maximum_fusion.1 = bf16[384,4,2304]{2,1,0:T(4,128)(2,1)} fusion(bf16[384,4,768]{2,1,0:T(4,128)(2,1)S(1)} %reshape.121, bf16[384,4,768]{2,1,0:T(4,128)(2,1)} %reshape.120, bf16[384,4,768]{2,1,0:T(4,128)(2,1)} %reshape.119), kind=kLoop, calls=%fused_computation.11 | loop fusion | flops 21233664 | bytes 14155776 | tf_op jit(solution)/shard_map/concatenate | solution.py:104
  40.3 18.0 %gather_fusion.3 = bf16[384,4,2304]{2,1,0:T(4,128)(2,1)} fusion(bf16[384,4,2304]{2,1,0:T(4,128)(2,1)} %pad_maximum_fusion.1, s32[1024]{0:T(1024)S(1)} %pad_clamp_fusion.3), kind=kCustom, calls=%fused_computation.3 | custom fusion | bytes 14157312 | tf_op jit(solution)/shard_map/gather | solution.py:112
  58.3 7.0 %copy.13 = bf16[8,48,4,2304]{3,1,2,0:T(8,128)(2,1)} copy(bf16[8,48,4,2304]{3,2,1,0:T(4,128)(2,1)} %bitcast.18) | data formatting | bytes 14155776 | tf_op jit(solution)/shard_map/reshape | solution.py:112
  65.3 5.9 %all-to-all-start = ((bf16[32,48,2304]{2,1,0:T(8,128)(2,1)}), bf16[32,48,2304]{2,1,0:T(8,128)(2,1)}, u32[]{:S(2)}, u32[]{:S(2)}) async-start(bf16[32,48,2304]{2,1,0:T(8,128)(2,1)} %bitcast.17), calls=%async_computation | async-start | bytes 14155776 | tf_op jit(solution)/shard_map/all_to_all | solution.py:118
  72.7 6.4 %scatter_custom_fusion = s32[1536]{0:T(1024)S(1)} fusion(s32[1536]{0:T(1024)S(1)} %fusion, s32[1536]{0:T(1024)S(1)} %iota.16, s32[]{:T(128)} %constant.15.clone.1), kind=kCustom, calls=%fused_computation.26 | custom fusion | bytes 6148 | tf_op jit(solution)/shard_map/scatter | solution.py:124
  79.1 149.4 %all-to-all-done = bf16[32,48,2304]{2,1,0:T(8,128)(2,1)} async-done(((bf16[32,48,2304]{2,1,0:T(8,128)(2,1)}), bf16[32,48,2304]{2,1,0:T(8,128)(2,1)}, u32[]{:S(2)}, u32[]{:S(2)}) %all-to-all-start) | async-done | bytes 7077920 | tf_op jit(solution)/shard_map/all_to_all | solution.py:118
  228.5 18.1 %gather_fusion.5 = bf16[1536,2304]{1,0:T(8,128)(2,1)} fusion(bf16[1536,2304]{1,0:T(8,128)(2,1)} %bitcast.5, s32[2048]{0:T(1024)S(1)} %pad_clamp_fusion.1), kind=kCustom, calls=%fused_computation.5 | custom fusion | bytes 14161920 | tf_op jit(solution)/shard_map/gather | solution.py:125
  246.6 5.4 %fusion.7 = (bf16[1152,1536]{1,0:T(8,128)(2,1)S(1)}, bf16[1152,1536]{1,0:T(8,128)(2,1)}) fusion(bf16[1536,2304]{1,0:T(8,128)(2,1)} %gather_fusion.5), kind=kLoop, calls=%fused_computation.34 | loop fusion | bytes 14155776 | tf_op jit(solution)/shard_map/slice | solution.py:131
  251.9 1.3 collective-permute-start.2
  253.2 6.3 %collective-permute-start.1 = (bf16[1152,1536]{1,0:T(8,128)(2,1)S(1)}, bf16[1152,1536]{1,0:T(8,128)(2,1)}, u32[]{:S(2)}, u32[]{:S(2)}) collective-permute-start(bf16[1152,1536]{1,0:T(8,128)(2,1)S(1)} %get-tuple-element.9), channel_id=1, source_target_pairs={{0,4},{4,12},{12,8},{8,16},{16,20},{20,28},{28,24},{1,5},{5,13},{1... | collective-permute-start | bytes 10616840 | tf_op jit(solution)/shard_map/ppermute | solution.py:131
  259.5 1.3 collective-permute-start
  261.5 0.7 gather_fusion
  263.4 1.2 gather_fusion.1
  264.6 0.7 pad_clamp_fusion
  265.3 3.2 slice.38.q_ref
  268.6 63.5 %collective-permute-done.2 = bf16[1152,1536]{1,0:T(8,128)(2,1)} collective-permute-done((bf16[1152,1536]{1,0:T(8,128)(2,1)}, bf16[1152,1536]{1,0:T(8,128)(2,1)}, u32[]{:S(2)}, u32[]{:S(2)}) %collective-permute-start.2) | collective-permute-done | bytes 3538976 | tf_op jit(solution)/shard_map/ppermute | solution.py:132
  332.1 0.9 collective-permute-done.1
  332.9 8.4 %pad_maximum_fusion.refs_0_.refs_1_.refs_2_.refs_3_.refs_4_.refs_5_.refs_6_.refs_7_ = bf16[3840,1536]{1,0:T(8,128)(2,1)} fusion(bf16[1152,1536]{1,0:T(8,128)(2,1)} %collective-permute-done.2, bf16[1536,1536]{1,0:T(8,128)(2,1)S(1)} %slice-done, bf16[1152,1536]{1,0:T(8,128)(2,1)} %collective-permute-done.1), kind=kLoop, calls=%fused_computation.10 | loop fusion | flops 35389440 | bytes 23592960 | tf_op jit(solution)/shard_map/concatenate | solution.py:133
  341.4 37.8 %shard_map.82 = bf16[1536,768]{1,0:T(8,128)(2,1)} custom-call(s32[16]{0:T(128)} %reshape.117.win_ref, s32[16]{0:T(128)} %gather_fusion.1, s32[4]{0:T(128)} %slice.17.vco_ref, bf16[1536,768]{1,0:T(8,128)(2,1)} %slice.38.q_ref, bf16[3840,1536]{1,0:T(8,128)(2,1)} %pad_maximum_fusion.refs_0_.refs_1_.refs_2_.refs_3_.refs_4_.refs_5_.refs_6_.refs_7_, ...), custom_call_target="tpu_custom_call" | custom-call | flops 7247757312 | bytes 23592960 | tf_op jit(solution)/shard_map/pallas_call | solution.py:68
  379.2 8.7 %gather_fusion.6 = bf16[1536,768]{1,0:T(8,128)(2,1)} fusion(bf16[1536,768]{1,0:T(8,128)(2,1)} %shard_map.82, s32[2048]{0:T(1024)S(1)} %pad_clamp_fusion), kind=kCustom, calls=%fused_computation.6 | custom fusion | bytes 4724736 | tf_op jit(solution)/shard_map/gather | solution.py:148
  387.9 14.1 %all-to-all-start.2 = ((bf16[32,48,768]{2,1,0:T(8,128)(2,1)}), bf16[32,48,768]{2,1,0:T(8,128)(2,1)S(1)}, u32[]{:S(2)}, u32[]{:S(2)}) async-start(bf16[32,48,768]{2,1,0:T(8,128)(2,1)} %bitcast.8), calls=%async_computation.2 | async-start | bytes 4718592 | tf_op jit(solution)/shard_map/all_to_all | solution.py:150
  402.0 3.0 scatter_custom_fusion.1
  405.1 51.3 %all-to-all-done.2 = bf16[32,48,768]{2,1,0:T(8,128)(2,1)S(1)} async-done(((bf16[32,48,768]{2,1,0:T(8,128)(2,1)}), bf16[32,48,768]{2,1,0:T(8,128)(2,1)S(1)}, u32[]{:S(2)}, u32[]{:S(2)}) %all-to-all-start.2) | async-done | bytes 2359328 | tf_op jit(solution)/shard_map/all_to_all | solution.py:150
  456.4 1.2 copy.14
  458.1 3.6 gather_fusion.7
  (40 shorter events, 4.6 us)
Async XLA Ops:
  0.0 261.5 %copy-start = (s32[32]{0:T(128)S(1)}, s32[32]{0:T(128)}, u32[]{:S(2)}) copy-start(s32[32]{0:T(128)} %param.13) | copy-start | bytes 388
  5.9 0.6 copy-start.3
  10.8 54.6 %all-to-all-start.1 = ((s32[32,1,48]{2,1,0:T(1,128)}), s32[32,1,48]{2,1,0:T(1,128)S(1)}, u32[]{:S(2)}, u32[]{:S(2)}) async-start(s32[32,1,48]{2,1,0:T(1,128)} %bitcast.6), calls=%async_computation.1 | async-start | bytes 32768 | tf_op jit(solution)/shard_map/all_to_all | solution.py:118
  65.3 6.0 %copy-start.4 = (s32[8]{0:T(128)S(1)}, s32[8]{0:T(128)}, u32[]{:S(2)}) copy-start(s32[8]{0:T(128)} %constant.38.clone) | copy-start | bytes 100
  65.3 163.2 %all-to-all-start = ((bf16[32,48,2304]{2,1,0:T(8,128)(2,1)}), bf16[32,48,2304]{2,1,0:T(8,128)(2,1)}, u32[]{:S(2)}, u32[]{:S(2)}) async-start(bf16[32,48,2304]{2,1,0:T(8,128)(2,1)} %bitcast.17), calls=%async_computation | async-start | bytes 14155776 | tf_op jit(solution)/shard_map/all_to_all | solution.py:118
  72.7 6.4 %copy-start.2 = (s32[1536]{0:T(1024)}, s32[1536]{0:T(1024)S(1)}, u32[]{:S(2)}) copy-start(s32[1536]{0:T(1024)S(1)} %fusion) | copy-start | bytes 18436
  251.9 80.2 %collective-permute-start.2 = (bf16[1152,1536]{1,0:T(8,128)(2,1)}, bf16[1152,1536]{1,0:T(8,128)(2,1)}, u32[]{:S(2)}, u32[]{:S(2)}) collective-permute-start(bf16[1152,1536]{1,0:T(8,128)(2,1)} %get-tuple-element.10), channel_id=1, source_target_pairs={{4,0},{12,4},{8,12},{16,8},{20,16},{28,20},{24,28},{5,1},{13,5},{9... | collective-permute-start | bytes 10616840 | tf_op jit(solution)/shard_map/ppermute | solution.py:132
  253.2 79.7 %collective-permute-start.1 = (bf16[1152,1536]{1,0:T(8,128)(2,1)S(1)}, bf16[1152,1536]{1,0:T(8,128)(2,1)}, u32[]{:S(2)}, u32[]{:S(2)}) collective-permute-start(bf16[1152,1536]{1,0:T(8,128)(2,1)S(1)} %get-tuple-element.9), channel_id=1, source_target_pairs={{0,4},{4,12},{12,8},{8,16},{16,20},{20,28},{28,24},{1,5},{5,13},{1... | collective-permute-start | bytes 10616840 | tf_op jit(solution)/shard_map/ppermute | solution.py:131
  259.5 3.2 collective-permute-start
  268.5 64.4 %slice-start = ((bf16[1536,2304]{1,0:T(8,128)(2,1)}), bf16[1536,1536]{1,0:T(8,128)(2,1)S(1)}, s32[]{:S(2)}) async-start(bf16[1536,2304]{1,0:T(8,128)(2,1)} %gather_fusion.5), calls=%async_computation.3 | async-start | bytes 9437184 | tf_op jit(solution)/shard_map/slice | solution.py:127
  387.9 68.6 %all-to-all-start.2 = ((bf16[32,48,768]{2,1,0:T(8,128)(2,1)}), bf16[32,48,768]{2,1,0:T(8,128)(2,1)S(1)}, u32[]{:S(2)}, u32[]{:S(2)}) async-start(bf16[32,48,768]{2,1,0:T(8,128)(2,1)} %bitcast.8), calls=%async_computation.2 | async-start | bytes 4718592 | tf_op jit(solution)/shard_map/all_to_all | solution.py:150
  458.1 3.6 copy-start.1
